TPU v7x, 128 devices: a whole 4x4x4 slice. The times are simulated.
128 devices in a mesh: dp: 32 (over z, x_lo, y), seq: 4 (over x_hi, core).
Axes of the slice: x: 4 (x_hi: 2, x_lo: 2; x = x_hi * 2 + x_lo), y: 4, z: 4, core: 2. Of those that a mesh axis runs over, the one named last changes fastest.
Arguments:
- queries: bfloat16 [32, 1024, 2560], P('dp', 'seq'), may hold values from -6 to 6
- keys_in: bfloat16 [32, 1024, 2560], P('dp', 'seq'), may hold values from -6 to 6
- values_in: bfloat16 [32, 1024, 2560], P('dp', 'seq'), may hold values from -6 to 6
- head_gain: float32 [20, 128], replicated, may hold values from 0.1 to 1.9
- master_weight: float32 [2560, 5120], P('dp', 'seq'), may hold values from -0.125 to 0.125
- gradient: float32 [2560, 5120], P('dp', 'seq'), may hold values from -6 to 6
- first_moment: float32 [2560, 5120], P('dp', 'seq'), may hold values from -4 to 4
- second_moment: float32 [2560, 5120], P('dp', 'seq'), may hold values from 0.01 to 4
Outputs:
- layer_out: bfloat16 [32, 1024, 5120], P('dp', 'seq')
- new_master: float32 [2560, 5120], P('dp', 'seq')
- new_first: float32 [2560, 5120], P('dp', 'seq')
- new_second: float32 [2560, 5120], P('dp', 'seq')
All inputs are finite; a program needn't handle non-finite values.
Results may differ from a plain program's by a relative error of at most 0.0061.
Values may be sent and summed in bfloat16 or wider, within the bound.
No kernel may reach another device: no remote copies, remote signals or barrier semaphores. Data moves between devices by JAX's collectives and lax.ppermute only.
A program may use at most 192 MiB of HBM per device.

v0:
```python
import math
import jax
import jax.numpy as jnp
from jax import lax
from jax.sharding import PartitionSpec as P

HEAD = 128
H = 20
CH = 128
beta_one = 0.9
beta_two = 0.95
learn_rate = 0.0003
decay_rate = 0.1
adam_eps = 1e-08
step_count = 100
norm_eps = 1e-06


def featurize(block, seq_length):
    positions = jnp.arange(block.shape[0], dtype=jnp.int32).astype(jnp.float32)
    angles = positions * (math.pi / (2.0 * seq_length))
    rectified = jnp.maximum(block.astype(jnp.float32), 0.0)
    cosine = rectified * jnp.cos(angles)[:, None, None]
    sine = rectified * jnp.sin(angles)[:, None, None]
    return jnp.concatenate([cosine, sine], axis=2).astype(jnp.bfloat16)


def block_states(key_feat, value_heads):
    blocks = key_feat.shape[0] // CH
    key_blocks = key_feat.reshape(blocks, CH, key_feat.shape[1], key_feat.shape[2])
    value_blocks = value_heads.reshape(blocks, CH, value_heads.shape[1], value_heads.shape[2])
    return jnp.einsum(
        "cjhf,cjhe->chfe", key_blocks, value_blocks, preferred_element_type=jnp.float32
    )


def attend(query_feat, key_feat, value_heads, states):
    count = query_feat.shape[0]
    heads_here = query_feat.shape[1]
    blocks = count // CH
    query_blocks = query_feat.reshape(blocks, CH, heads_here, 2 * HEAD)
    key_blocks = key_feat.reshape(blocks, CH, heads_here, 2 * HEAD)
    value_blocks = value_heads.reshape(blocks, CH, heads_here, HEAD)
    scores = jnp.einsum(
        "cihf,cjhf->chij", query_blocks, key_blocks, preferred_element_type=jnp.float32
    )
    causal_mask = jnp.arange(CH)[:, None] >= jnp.arange(CH)[None, :]
    scores = jnp.where(causal_mask[None, None], scores, 0.0).astype(jnp.bfloat16)
    inside_block = jnp.einsum(
        "chij,cjhe->cihe", scores, value_blocks, preferred_element_type=jnp.float32
    )
    running = jnp.cumsum(states, axis=0)
    before = jnp.concatenate([jnp.zeros_like(states[:1]), running[:-1]], axis=0)
    before = before.astype(jnp.bfloat16)
    from_before = jnp.einsum(
        "cihf,chfe->cihe", query_blocks, before, preferred_element_type=jnp.float32
    )
    return (inside_block + from_before).reshape(count, heads_here, HEAD)


def normalize(attended, gain_rows):
    mean_square = jnp.mean(attended * attended, axis=2, keepdims=True)
    return (attended * lax.rsqrt(mean_square + norm_eps) * gain_rows[None]).astype(jnp.bfloat16)


def on_device(
    queries, keys_in, values_in, head_gain, master_weight, gradient, first_moment, second_moment
):
    moment_one = beta_one * first_moment + (1.0 - beta_one) * gradient
    moment_two = beta_two * second_moment + (1.0 - beta_two) * gradient * gradient
    corrected = (
        moment_one
        / (1.0 - beta_one**step_count)
        / (jnp.sqrt(moment_two / (1.0 - beta_two**step_count)) + adam_eps)
    )
    updated = master_weight - learn_rate * (corrected + decay_rate * master_weight)
    weights = updated.astype(jnp.bfloat16)
    tokens_here = queries.shape[1]
    seq_length = tokens_here * lax.axis_size("seq")
    query_heads = queries[0].reshape(tokens_here, H, HEAD)
    key_heads = keys_in[0].reshape(tokens_here, H, HEAD)
    value_heads = values_in[0].reshape(tokens_here, H, HEAD)
    query_group, key_group, value_group = (
        lax.all_to_all(query_heads, "seq", split_axis=1, concat_axis=0, tiled=True),
        lax.all_to_all(key_heads, "seq", split_axis=1, concat_axis=0, tiled=True),
        lax.all_to_all(value_heads, "seq", split_axis=1, concat_axis=0, tiled=True),
    )
    heads_here = query_group.shape[1]
    query_feat = featurize(query_group, seq_length)
    key_feat = featurize(key_group, seq_length)
    states = block_states(key_feat, value_group)
    attended = attend(query_feat, key_feat, value_group, states)
    gain_rows = lax.dynamic_slice_in_dim(
        head_gain, lax.axis_index("seq") * heads_here, heads_here, 0
    )
    normed_group = normalize(attended, gain_rows)
    normed_all = lax.all_gather(normed_group, "seq", axis=1, tiled=True)
    normed_all = normed_all.reshape(normed_all.shape[0], H * HEAD)
    cols = lax.all_gather(weights, "dp", axis=0, tiled=True)
    part = jnp.dot(normed_all, cols, preferred_element_type=jnp.float32).astype(jnp.bfloat16)
    projected = lax.all_to_all(part, "seq", split_axis=0, concat_axis=1, tiled=True)
    layer_out = projected[None]
    return (layer_out, updated, moment_one, moment_two)


def solution(mesh):
    in_specs = (
        P("dp", "seq", None),
        P("dp", "seq", None),
        P("dp", "seq", None),
        P(),
        P("dp", "seq"),
        P("dp", "seq"),
        P("dp", "seq"),
        P("dp", "seq"),
    )
    out_specs = (P("dp", "seq", None), P("dp", "seq"), P("dp", "seq"), P("dp", "seq"))
    return jax.shard_map(
        on_device, mesh=mesh, in_specs=in_specs, out_specs=out_specs, check_vma=False
    )
```

profile of v0, /device:TPU:1, one launch (start us, length us, event | category | flops | bytes accessed | tf_op | source)
XLA Modules:
  0.0 368.6 jit_solution(1960539132442733777)
XLA Ops:
  7.2 2.5 copy.30
  9.7 5.8 %all-to-all-start = ((bf16[256,20,128]{0,2,1:T(8,128)(2,1)}), bf16[256,20,128]{0,2,1:T(8,128)(2,1)S(1)}, u32[]{:S(2)}, u32[]{:S(2)}) async-start(bf16[256,20,128]{0,2,1:T(8,128)(2,1)} %bitcast), calls=%async_computation | async-start | bytes 2621440 | tf_op jit(solution)/shard_map/all_to_all | solution.py:84
  17.0 16.5 %all-to-all-done = bf16[256,20,128]{0,2,1:T(8,128)(2,1)S(1)} async-done(((bf16[256,20,128]{0,2,1:T(8,128)(2,1)}), bf16[256,20,128]{0,2,1:T(8,128)(2,1)S(1)}, u32[]{:S(2)}, u32[]{:S(2)}) %all-to-all-start) | async-done | bytes 1310752 | tf_op jit(solution)/shard_map/all_to_all | solution.py:84
  33.4 4.4 %all-to-all-start.1 = ((bf16[256,20,128]{0,2,1:T(8,128)(2,1)}), bf16[256,20,128]{0,2,1:T(8,128)(2,1)S(1)}, u32[]{:S(2)}, u32[]{:S(2)}) async-start(bf16[256,20,128]{0,2,1:T(8,128)(2,1)} %bitcast.5), calls=%async_computation.1 | async-start | bytes 2621440 | tf_op jit(solution)/shard_map/all_to_all | solution.py:85
  37.8 2.4 copy.40
  40.2 15.5 %all-to-all-done.1 = bf16[256,20,128]{0,2,1:T(8,128)(2,1)S(1)} async-done(((bf16[256,20,128]{0,2,1:T(8,128)(2,1)}), bf16[256,20,128]{0,2,1:T(8,128)(2,1)S(1)}, u32[]{:S(2)}, u32[]{:S(2)}) %all-to-all-start.1) | async-done | bytes 1310752 | tf_op jit(solution)/shard_map/all_to_all | solution.py:85
  55.7 5.1 %all-to-all-start.2 = ((bf16[256,20,128]{0,2,1:T(8,128)(2,1)}), bf16[256,20,128]{0,2,1:T(8,128)(2,1)}, u32[]{:S(2)}, u32[]{:S(2)}) async-start(bf16[256,20,128]{0,2,1:T(8,128)(2,1)} %bitcast.10), calls=%async_computation.2 | async-start | bytes 2621440 | tf_op jit(solution)/shard_map/all_to_all | solution.py:86
  60.9 1.6 convert_maximum_fusion.1
  62.5 2.1 copy.32
  64.6 1.6 convert_maximum_fusion
  66.2 2.1 copy.37
  68.3 10.6 %all-to-all-done.2 = bf16[256,20,128]{0,2,1:T(8,128)(2,1)} async-done(((bf16[256,20,128]{0,2,1:T(8,128)(2,1)}), bf16[256,20,128]{0,2,1:T(8,128)(2,1)}, u32[]{:S(2)}, u32[]{:S(2)}) %all-to-all-start.2) | async-done | bytes 1310752 | tf_op jit(solution)/shard_map/all_to_all | solution.py:86
  78.9 2.4 copy.42
  81.3 3.7 multiply_convert_fusion.1
  88.1 5.6 %fusion.7 = f32[8,5,128,128]{3,2,1,0:T(8,128)} fusion(bf16[8,128,5,128]{3,1,2,0:T(8,128)(2,1)} %copy-done.4, bf16[8,128,5,128]{3,1,2,0:T(8,128)(2,1)} %copy-done.3, bf16[8,128,5,128]{3,1,2,0:T(8,128)(2,1)} %get-tuple-element.12, bf16[8,128,5,128]{3,1,2,0:T(8,128)(2,1)} %get-tuple-element.13, pred[128,128]{1,0:T(8,128)(4,1)S(1)} %iota_compare_fusion, ...), kind=kOutput, calls=%fused_computation.19 | convolution fusion | flops 515112960 | bytes 9191424 | tf_op jit(solution)/shard_map/chij,cjhe->cihe/dot_general | solution.py:49
  93.7 3.5 multiply_reduce_fusion
  97.6 1.9 fusion.1
  100.9 43.9 %all-gather.3.cloned.1.call-done = bf16[1024,20,128]{2,0,1:T(8,128)(2,1)} async-done(((bf16[1024,5,128]{2,0,1:T(8,128)(2,1)}), bf16[1024,20,128]{2,0,1:T(8,128)(2,1)}) %all-gather.3.cloned.1.call-update) | async-done | bytes 5242896 | tf_op jit(solution)/shard_map/all_gather | solution.py:97
  144.8 7.9 %copy.47 = bf16[1024,20,128]{0,2,1:T(8,128)(2,1)} copy(bf16[1024,20,128]{2,0,1:T(8,128)(2,1)} %all-gather.3.cloned.1.call-done) | data formatting | bytes 10485760 | tf_op jit(solution)/shard_map/all_gather | solution.py:97
  152.7 136.5 %all-gather.5.cloned.1.call-done = bf16[2560,1280]{1,0:T(8,128)(2,1)} async-done(((bf16[80,1280]{1,0:T(8,128)(2,1)}), bf16[2560,1280]{1,0:T(8,128)(2,1)}) %all-gather.5.cloned.1.call-update) | async-done | bytes 6553616 | tf_op jit(solution)/shard_map/all_gather | solution.py:99
  289.2 10.9 %convolution_convert_fusion = bf16[1024,1280]{1,0:T(8,128)(2,1)S(1)} fusion(bf16[1024,2560]{0,1:T(8,128)(2,1)} %bitcast.40, bf16[2560,1280]{1,0:T(8,128)(2,1)} %all-gather.5.cloned.1.call-done), kind=kOutput, calls=%fused_computation.1 | convolution fusion | flops 6712197120 | bytes 14417920 | tf_op jit(solution)/shard_map/dot_general | solution.py:100
  300.2 56.4 %all_to_all.49 = bf16[4,256,1280]{2,1,0:T(8,128)(2,1)S(1)} all-to-all(bf16[4,256,1280]{2,1,0:T(8,128)(2,1)S(1)} %bitcast.41), channel_id=1, replica_groups=mesh['dp'=32,'seq'=4] {'seq'}, dimensions={0} | all-to-all | bytes 5242880 | tf_op jit(solution)/shard_map/all_to_all | solution.py:101
  356.6 2.0 copy.48
  358.6 3.2 broadcast_in_dim.16
  (40 shorter events, 6.3 us)
Async XLA Ops:
  7.2 53.7 %copy-start = (f32[20,128]{1,0:T(8,128)S(1)}, f32[20,128]{1,0:T(8,128)}, u32[]{:S(2)}) copy-start(f32[20,128]{1,0:T(8,128)} %param.11) | copy-start | bytes 30724
  7.2 8.3 %copy-start.8 = (bf16[1,256,2560]{2,1,0:T(8,128)(2,1)S(1)}, bf16[1,256,2560]{2,1,0:T(8,128)(2,1)}, u32[]{:S(2)}) copy-start(bf16[1,256,2560]{2,1,0:T(8,128)(2,1)} %param.9) | copy-start | bytes 3932164
  9.7 23.7 %all-to-all-start = ((bf16[256,20,128]{0,2,1:T(8,128)(2,1)}), bf16[256,20,128]{0,2,1:T(8,128)(2,1)S(1)}, u32[]{:S(2)}, u32[]{:S(2)}) async-start(bf16[256,20,128]{0,2,1:T(8,128)(2,1)} %bitcast), calls=%async_computation | async-start | bytes 2621440 | tf_op jit(solution)/shard_map/all_to_all | solution.py:84
  33.4 6.8 %copy-start.6 = (bf16[256,20,128]{0,2,1:T(8,128)(2,1)}, bf16[256,20,128]{0,2,1:T(8,128)(2,1)S(1)}, u32[]{:S(2)}) copy-start(bf16[256,20,128]{0,2,1:T(8,128)(2,1)S(1)} %all-to-all-done) | copy-start | bytes 3932164
  33.4 22.3 %all-to-all-start.1 = ((bf16[256,20,128]{0,2,1:T(8,128)(2,1)}), bf16[256,20,128]{0,2,1:T(8,128)(2,1)S(1)}, u32[]{:S(2)}, u32[]{:S(2)}) async-start(bf16[256,20,128]{0,2,1:T(8,128)(2,1)} %bitcast.5), calls=%async_computation.1 | async-start | bytes 2621440 | tf_op jit(solution)/shard_map/all_to_all | solution.py:85
  55.7 5.2 %copy-start.7 = (bf16[256,20,128]{0,2,1:T(8,128)(2,1)}, bf16[256,20,128]{0,2,1:T(8,128)(2,1)S(1)}, u32[]{:S(2)}) copy-start(bf16[256,20,128]{0,2,1:T(8,128)(2,1)S(1)} %all-to-all-done.1) | copy-start | bytes 3932164
  55.7 23.1 %all-to-all-start.2 = ((bf16[256,20,128]{0,2,1:T(8,128)(2,1)}), bf16[256,20,128]{0,2,1:T(8,128)(2,1)}, u32[]{:S(2)}, u32[]{:S(2)}) async-start(bf16[256,20,128]{0,2,1:T(8,128)(2,1)} %bitcast.10), calls=%async_computation.2 | async-start | bytes 2621440 | tf_op jit(solution)/shard_map/all_to_all | solution.py:86
  60.9 83.9 %all-gather.3.cloned.1.call-start = ((), (), s32[]{:S(2)}) async-start(), calls=%async_computation.4 | async-start | bytes 6553600 | tf_op jit(solution)/shard_map/all_gather | solution.py:97
  68.3 13.0 %copy-start.2 = (f32[4,256,5,128]{3,1,0,2:T(8,128)S(1)}, f32[4,256,5,128]{3,1,0,2:T(8,128)}, u32[]{:S(2)}) copy-start(f32[4,256,5,128]{3,1,0,2:T(8,128)} %copy.32) | copy-start | bytes 7864324
  81.3 5.2 %copy-start.5 = (bf16[4,256,5,128]{3,1,0,2:T(8,128)(2,1)S(1)}, bf16[4,256,5,128]{3,1,0,2:T(8,128)(2,1)}, u32[]{:S(2)}) copy-start(bf16[4,256,5,128]{3,1,0,2:T(8,128)(2,1)} %copy.42) | copy-start | bytes 3932164
  85.0 1.1 copy-start.3
  85.0 1.5 copy-start.4
  97.6 2.0 copy-start.9
  97.6 2.0 copy-start.10
  97.6 2.0 copy-start.11
  97.6 2.0 copy-start.12
  99.5 189.7 %all-gather.5.cloned.1.call-start = ((), (), s32[]{:S(2)}) async-start(), calls=%async_computation.5 | async-start | bytes 6758400 | tf_op jit(solution)/shard_map/all_gather | solution.py:99
  356.6 5.2 %copy-start.1 = (f32[20,128]{1,0:T(8,128)S(1)}, f32[20,128]{1,0:T(8,128)}, u32[]{:S(2)}) copy-start(f32[20,128]{1,0:T(8,128)} %param.11) | copy-start | bytes 30724
Sparse Core Ops, SparseCore 0:
  99.6 45.1 all-gather.2
  146.4 142.7 all-gather.4
where the time goes:
time: 369 us
  waiting for transfers between devices  223 us (60%)
  blocking collectives  56.4 us (15%)
  local copies, waits for them, and re-layouts  28 us (8%)
  matrix products  20.9 us (6%)
  starting transfers between devices  15.3 us (4%)
  between operations  14.2 us (4%)
  other arithmetic  10.7 us (3%)
    all_gather x1, waiting for transfers between devices, on_device(): cols = lax.all_gather(weights, 'dp', axis=0, tiled=True)  137 us
    all_to_all x1, blocking collectives, on_device(): lax.all_to_all(part, 'seq', split_axis=0, concat_axis=1, tiled=True)  56.4 us
    all_gather x1, waiting for transfers between devices, on_device(): normed_all = lax.all_gather(normed_group, 'seq', axis=1, tiled=True)  43.9 us
    all_to_all x1, waiting for transfers between devices, on_device(): lax.all_to_all(query_heads, 'seq', split_axis=1, concat_axis=0, tiled=True)  16.5 us
    all_to_all x1, waiting for transfers between devices, on_device(): lax.all_to_all(key_heads, 'seq', split_axis=1, concat_axis=0, tiled=True)  15.5 us
    dot_general x1, matrix products, on_device(): jnp.dot(normed_all, cols, preferred_element_type=jnp.float32)  10.9 us
    all_to_all x1, waiting for transfers between devices, on_device(): lax.all_to_all(value_heads, 'seq', split_axis=1, concat_axis=0, tiled=True)  10.6 us
    all_gather x1, local copies, waits for them, and re-layouts, on_device(): normed_all = lax.all_gather(normed_group, 'seq', axis=1, tiled=True)  7.92 us
  transfers between devices with their start and end apart: 5, of which 5 were waited for; matrix products, arithmetic and copies ran while one was open for 6% of the time, Pallas kernels for 0%

commit v1 on v0

--- a/solution.py
+++ b/solution.py
@@ -96,7 +96,9 @@
     normed_group = normalize(attended, gain_rows)
     normed_all = lax.all_gather(normed_group, "seq", axis=1, tiled=True)
     normed_all = normed_all.reshape(normed_all.shape[0], H * HEAD)
-    cols = lax.all_gather(weights, "dp", axis=0, tiled=True)
+    cols = jnp.concatenate(
+        lax.all_to_all(jnp.stack([weights] * lax.axis_size("dp")), "dp", 0, 0), axis=0
+    )
     part = jnp.dot(normed_all, cols, preferred_element_type=jnp.float32).astype(jnp.bfloat16)
     projected = lax.all_to_all(part, "seq", split_axis=0, concat_axis=1, tiled=True)
     layer_out = projected[None]

time: 369 us -> 289 us (0.78)
  the two profiles are of different devices: /device:TPU:1 before, /device:TPU:48 now
where the time goes in v1:
time: 289 us; the launch traced here: 288 us
  waiting for transfers between devices  152 us (53%)
  blocking collectives  38.5 us (13%)
  local copies, waits for them, and re-layouts  31.3 us (11%)
  matrix products  20.9 us (7%)
  starting transfers between devices  20.4 us (7%)
  between operations  14.2 us (5%)
  other arithmetic  10.6 us (4%)
    all_gather x1, waiting for transfers between devices, on_device(): normed_all = lax.all_gather(normed_group, 'seq', axis=1, tiled=True)  61.8 us
    all_to_all x1, waiting for transfers between devices, on_device(): lax.all_to_all(jnp.stack([weights] * lax.axis_size('dp')), 'dp', 0, 0)  45.2 us
    all_to_all x1, blocking collectives, on_device(): lax.all_to_all(part, 'seq', split_axis=0, concat_axis=1, tiled=True)  38.5 us
    all_to_all x1, waiting for transfers between devices, on_device(): lax.all_to_all(query_heads, 'seq', split_axis=1, concat_axis=0, tiled=True)  17.3 us
    all_to_all x1, waiting for transfers between devices, on_device(): lax.all_to_all(key_heads, 'seq', split_axis=1, concat_axis=0, tiled=True)  16.3 us
    all_to_all x1, waiting for transfers between devices, on_device(): lax.all_to_all(value_heads, 'seq', split_axis=1, concat_axis=0, tiled=True)  11.3 us
    dot_general x1, matrix products, on_device(): jnp.dot(normed_all, cols, preferred_element_type=jnp.float32)  10.9 us
    all_to_all x1, starting transfers between devices, on_device(): lax.all_to_all(jnp.stack([weights] * lax.axis_size('dp')), 'dp', 0, 0)  8.19 us
  transfers between devices with their start and end apart: 5, of which 5 were waited for; matrix products, arithmetic and copies ran while one was open for 8% of the time, Pallas kernels for 0%

profile of v1, /device:TPU:48, one launch (start us, length us, event | category | flops | bytes accessed | tf_op | source)
XLA Modules:
  0.0 287.9 jit_solution(4932504594030135636)
XLA Ops:
  7.2 2.5 copy.30
  9.7 4.3 %all-to-all-start = ((bf16[256,20,128]{0,2,1:T(8,128)(2,1)}), bf16[256,20,128]{0,2,1:T(8,128)(2,1)S(1)}, u32[]{:S(2)}, u32[]{:S(2)}) async-start(bf16[256,20,128]{0,2,1:T(8,128)(2,1)} %bitcast), calls=%async_computation | async-start | bytes 2621440 | tf_op jit(solution)/shard_map/all_to_all | solution.py:84
  15.4 17.3 %all-to-all-done = bf16[256,20,128]{0,2,1:T(8,128)(2,1)S(1)} async-done(((bf16[256,20,128]{0,2,1:T(8,128)(2,1)}), bf16[256,20,128]{0,2,1:T(8,128)(2,1)S(1)}, u32[]{:S(2)}, u32[]{:S(2)}) %all-to-all-start) | async-done | bytes 1310752 | tf_op jit(solution)/shard_map/all_to_all | solution.py:84
  32.8 3.5 %all-to-all-start.1 = ((bf16[256,20,128]{0,2,1:T(8,128)(2,1)}), bf16[256,20,128]{0,2,1:T(8,128)(2,1)S(1)}, u32[]{:S(2)}, u32[]{:S(2)}) async-start(bf16[256,20,128]{0,2,1:T(8,128)(2,1)} %bitcast.5), calls=%async_computation.1 | async-start | bytes 2621440 | tf_op jit(solution)/shard_map/all_to_all | solution.py:85
  36.3 2.4 copy.40
  38.8 16.3 %all-to-all-done.1 = bf16[256,20,128]{0,2,1:T(8,128)(2,1)S(1)} async-done(((bf16[256,20,128]{0,2,1:T(8,128)(2,1)}), bf16[256,20,128]{0,2,1:T(8,128)(2,1)S(1)}, u32[]{:S(2)}, u32[]{:S(2)}) %all-to-all-start.1) | async-done | bytes 1310752 | tf_op jit(solution)/shard_map/all_to_all | solution.py:85
  55.1 4.3 %all-to-all-start.2 = ((bf16[256,20,128]{0,2,1:T(8,128)(2,1)}), bf16[256,20,128]{0,2,1:T(8,128)(2,1)}, u32[]{:S(2)}, u32[]{:S(2)}) async-start(bf16[256,20,128]{0,2,1:T(8,128)(2,1)} %bitcast.10), calls=%async_computation.2 | async-start | bytes 2621440 | tf_op jit(solution)/shard_map/all_to_all | solution.py:86
  61.1 2.1 copy.32
  64.8 2.1 copy.37
  66.9 11.3 %all-to-all-done.2 = bf16[256,20,128]{0,2,1:T(8,128)(2,1)} async-done(((bf16[256,20,128]{0,2,1:T(8,128)(2,1)}), bf16[256,20,128]{0,2,1:T(8,128)(2,1)}, u32[]{:S(2)}, u32[]{:S(2)}) %all-to-all-start.2) | async-done | bytes 1310752 | tf_op jit(solution)/shard_map/all_to_all | solution.py:86
  78.2 2.4 copy.42
  80.6 3.7 %multiply_convert_fusion.1 = (bf16[8,128,5,128]{3,1,2,0:T(8,128)(2,1)S(1)}, bf16[8,128,5,128]{3,1,2,0:T(8,128)(2,1)S(1)}, bf16[8,128,5,128]{3,1,2,0:T(8,128)(2,1)}, bf16[8,128,5,128]{3,1,2,0:T(8,128)(2,1)}) fusion(f32[8,128,5,128]{3,1,0,2:T(8,128)} %bitcast.38, f32[8,128]{1,0:T(8,128)S(1)} %get-tuple-element.17, f32[8,128]{1,0:T(8,128)S(1)} %get-tuple-element.16, ...), kind=kLoop, calls=%fused_computation.13 | loop fusion | flops 5242880 | bytes 10493952 | tf_op jit(solution)/shard_map/convert.3
  87.5 5.6 %fusion.7 = f32[8,5,128,128]{3,2,1,0:T(8,128)} fusion(bf16[8,128,5,128]{3,1,2,0:T(8,128)(2,1)} %copy-done.4, bf16[8,128,5,128]{3,1,2,0:T(8,128)(2,1)} %copy-done.3, bf16[8,128,5,128]{3,1,2,0:T(8,128)(2,1)} %get-tuple-element.12, bf16[8,128,5,128]{3,1,2,0:T(8,128)(2,1)} %get-tuple-element.13, pred[128,128]{1,0:T(8,128)(4,1)S(1)} %iota_compare_fusion, ...), kind=kOutput, calls=%fused_computation.19 | convolution fusion | flops 515112960 | bytes 9191424 | tf_op jit(solution)/shard_map/chij,cjhe->cihe/dot_general | solution.py:49
  93.1 3.5 %multiply_reduce_fusion = (f32[8,128,5]{1,2,0:T(8,128)S(1)}, f32[8,128,5,128]{3,1,2,0:T(8,128)S(1)}) fusion(bf16[7,5,256,128]{3,2,1,0:T(8,128)(2,1)S(1)} %slice.7, bf16[8,128,5,128]{3,1,2,0:T(8,128)(2,1)} %get-tuple-element.12, bf16[8,128,5,128]{3,1,2,0:T(8,128)(2,1)} %get-tuple-element.13, f32[8,5,128,128]{3,2,1,0:T(8,128)} %fusion.7), kind=kOutput, calls=%fused_computation.8 | convolution fusion | flops 342748160 | bytes 10178560 | tf_op jit(solution)/shard_map/cihf,chfe->cihe/dot_general | solution.py:55
  97.0 1.9 fusion.1
  100.1 3.2 %stack.2 = bf16[32,80,1280]{2,1,0:T(8,128)(2,1)} broadcast(bf16[80,1280]{1,0:T(8,128)(2,1)S(1)} %get-tuple-element.4), dimensions={1,2} | broadcast | bytes 6758400 | tf_op jit(solution)/shard_map/stack | solution.py:100
  103.3 8.2 %all-to-all-start.3 = ((bf16[32,80,1280]{2,1,0:T(8,128)(2,1)}), bf16[32,80,1280]{2,1,0:T(8,128)(2,1)}, u32[]{:S(2)}, u32[]{:S(2)}) async-start(bf16[32,80,1280]{2,1,0:T(8,128)(2,1)} %stack.2), calls=%async_computation.3 | async-start | bytes 13107200 | tf_op jit(solution)/shard_map/all_to_all | solution.py:100
  111.5 61.8 %all-gather.2.cloned.1.call-done = bf16[1024,20,128]{2,0,1:T(8,128)(2,1)} async-done(((bf16[1024,5,128]{2,0,1:T(8,128)(2,1)}), bf16[1024,20,128]{2,0,1:T(8,128)(2,1)}) %all-gather.2.cloned.1.call-update) | async-done | bytes 5242896 | tf_op jit(solution)/shard_map/all_gather | solution.py:97
  173.4 7.9 %copy.47 = bf16[1024,20,128]{0,2,1:T(8,128)(2,1)} copy(bf16[1024,20,128]{2,0,1:T(8,128)(2,1)} %all-gather.2.cloned.1.call-done) | data formatting | bytes 10485760 | tf_op jit(solution)/shard_map/all_gather | solution.py:97
  181.3 45.2 %all-to-all-done.3 = bf16[32,80,1280]{2,1,0:T(8,128)(2,1)} async-done(((bf16[32,80,1280]{2,1,0:T(8,128)(2,1)}), bf16[32,80,1280]{2,1,0:T(8,128)(2,1)}, u32[]{:S(2)}, u32[]{:S(2)}) %all-to-all-start.3) | async-done | bytes 6553632 | tf_op jit(solution)/shard_map/all_to_all | solution.py:100
  226.5 10.9 %convolution_convert_fusion = bf16[1024,1280]{1,0:T(8,128)(2,1)S(1)} fusion(bf16[1024,2560]{0,1:T(8,128)(2,1)} %bitcast.41, bf16[2560,1280]{1,0:T(8,128)(2,1)} %bitcast.20), kind=kOutput, calls=%fused_computation.1 | convolution fusion | flops 6712197120 | bytes 14417920 | tf_op jit(solution)/shard_map/dot_general | solution.py:102
  237.4 38.5 %all_to_all.54 = bf16[4,256,1280]{2,1,0:T(8,128)(2,1)S(1)} all-to-all(bf16[4,256,1280]{2,1,0:T(8,128)(2,1)S(1)} %bitcast.42), channel_id=1, replica_groups=mesh['dp'=32,'seq'=4] {'seq'}, dimensions={0} | all-to-all | bytes 5242880 | tf_op jit(solution)/shard_map/all_to_all | solution.py:103
  275.8 2.0 copy.48
  277.9 3.2 %broadcast_in_dim.16 = bf16[1,256,5120]{2,1,0:T(8,128)(2,1)} reshape(bf16[256,4,1280]{2,1,0:T(4,128)(2,1)S(1)} %copy.48) | data formatting | bytes 5242880 | tf_op jit(solution)/shard_map/broadcast_in_dim | solution.py:104
  (40 shorter events, 9.4 us)
Async XLA Ops:
  7.2 52.3 %copy-start = (f32[20,128]{1,0:T(8,128)S(1)}, f32[20,128]{1,0:T(8,128)}, u32[]{:S(2)}) copy-start(f32[20,128]{1,0:T(8,128)} %param.11) | copy-start | bytes 30724
  7.2 6.8 %copy-start.8 = (bf16[1,256,2560]{2,1,0:T(8,128)(2,1)S(1)}, bf16[1,256,2560]{2,1,0:T(8,128)(2,1)}, u32[]{:S(2)}) copy-start(bf16[1,256,2560]{2,1,0:T(8,128)(2,1)} %param.9) | copy-start | bytes 3932164
  9.7 23.1 %all-to-all-start = ((bf16[256,20,128]{0,2,1:T(8,128)(2,1)}), bf16[256,20,128]{0,2,1:T(8,128)(2,1)S(1)}, u32[]{:S(2)}, u32[]{:S(2)}) async-start(bf16[256,20,128]{0,2,1:T(8,128)(2,1)} %bitcast), calls=%async_computation | async-start | bytes 2621440 | tf_op jit(solution)/shard_map/all_to_all | solution.py:84
  32.8 6.0 %copy-start.6 = (bf16[256,20,128]{0,2,1:T(8,128)(2,1)}, bf16[256,20,128]{0,2,1:T(8,128)(2,1)S(1)}, u32[]{:S(2)}) copy-start(bf16[256,20,128]{0,2,1:T(8,128)(2,1)S(1)} %all-to-all-done) | copy-start | bytes 3932164
  32.8 22.3 %all-to-all-start.1 = ((bf16[256,20,128]{0,2,1:T(8,128)(2,1)}), bf16[256,20,128]{0,2,1:T(8,128)(2,1)S(1)}, u32[]{:S(2)}, u32[]{:S(2)}) async-start(bf16[256,20,128]{0,2,1:T(8,128)(2,1)} %bitcast.5), calls=%async_computation.1 | async-start | bytes 2621440 | tf_op jit(solution)/shard_map/all_to_all | solution.py:85
  55.1 4.4 %copy-start.7 = (bf16[256,20,128]{0,2,1:T(8,128)(2,1)}, bf16[256,20,128]{0,2,1:T(8,128)(2,1)S(1)}, u32[]{:S(2)}) copy-start(bf16[256,20,128]{0,2,1:T(8,128)(2,1)S(1)} %all-to-all-done.1) | copy-start | bytes 3932164
  55.1 23.1 %all-to-all-start.2 = ((bf16[256,20,128]{0,2,1:T(8,128)(2,1)}), bf16[256,20,128]{0,2,1:T(8,128)(2,1)}, u32[]{:S(2)}, u32[]{:S(2)}) async-start(bf16[256,20,128]{0,2,1:T(8,128)(2,1)} %bitcast.10), calls=%async_computation.2 | async-start | bytes 2621440 | tf_op jit(solution)/shard_map/all_to_all | solution.py:86
  59.4 114.0 %all-gather.2.cloned.1.call-start = ((), (), s32[]{:S(2)}) async-start(), calls=%async_computation.5 | async-start | bytes 6553600 | tf_op jit(solution)/shard_map/all_gather | solution.py:97
  66.9 13.8 %copy-start.2 = (f32[4,256,5,128]{3,1,0,2:T(8,128)S(1)}, f32[4,256,5,128]{3,1,0,2:T(8,128)}, u32[]{:S(2)}) copy-start(f32[4,256,5,128]{3,1,0,2:T(8,128)} %copy.32) | copy-start | bytes 7864324
  80.6 5.2 %copy-start.5 = (bf16[4,256,5,128]{3,1,0,2:T(8,128)(2,1)S(1)}, bf16[4,256,5,128]{3,1,0,2:T(8,128)(2,1)}, u32[]{:S(2)}) copy-start(bf16[4,256,5,128]{3,1,0,2:T(8,128)(2,1)} %copy.42) | copy-start | bytes 3932164
  84.3 1.1 copy-start.3
  84.3 1.5 copy-start.4
  96.9 1.9 copy-start.9
  96.9 1.9 copy-start.10
  97.0 1.9 copy-start.11
  97.0 1.9 copy-start.12
  103.3 123.1 %all-to-all-start.3 = ((bf16[32,80,1280]{2,1,0:T(8,128)(2,1)}), bf16[32,80,1280]{2,1,0:T(8,128)(2,1)}, u32[]{:S(2)}, u32[]{:S(2)}) async-start(bf16[32,80,1280]{2,1,0:T(8,128)(2,1)} %stack.2), calls=%async_computation.3 | async-start | bytes 13107200 | tf_op jit(solution)/shard_map/all_to_all | solution.py:100
  275.8 5.2 %copy-start.1 = (f32[20,128]{1,0:T(8,128)S(1)}, f32[20,128]{1,0:T(8,128)}, u32[]{:S(2)}) copy-start(f32[20,128]{1,0:T(8,128)} %param.11) | copy-start | bytes 30724
Sparse Core Ops, SparseCore 0:
  99.0 74.3 all-gather.1
